TPU v7x, 32 devices: a whole 2x2x4 slice. The times are simulated.
32 devices in a mesh: groups: 2 (over y), lat: 8 (over z, x), seed: 2 (over core).
Axes of the slice: x: 2, y: 2, z: 4, core: 2. Of those that a mesh axis runs over, the one named last changes fastest.
Arguments:
- activations: bfloat16 [512, 2048], P(('groups', 'seed'), 'lat'), parts along dimension 0, may hold values from -6 to 6
- bag_rows: int32 [4, 256], P(('groups', 'seed')), parts along dimension 0, may hold values from 0 to 255
- keep_cols: int32 [4, 2048], P(('groups', 'seed')), parts along dimension 0, may hold values 0 or 1
- enc_weight: bfloat16 [4, 16384, 2048], P(('groups', 'seed'), 'lat'), parts along dimension 0, may hold values from -0.125 to 0.125
- enc_bias: float32 [4, 16384], P(('groups', 'seed'), 'lat'), parts along dimension 0, may hold values from -3 to 3
- dec_weight: bfloat16 [4, 16384, 2048], P(('groups', 'seed'), 'lat'), parts along dimension 0, may hold values from -0.0625 to 0.0625
- dec_bias: float32 [4, 2048], P(('groups', 'seed')), parts along dimension 0, may hold values from -3 to 3
- first_moment: bfloat16 [4, 16384, 2048], P(('groups', 'seed'), 'lat'), parts along dimension 0, may hold values from -0.3125 to 0.3125
- second_moment: bfloat16 [4, 16384, 2048], P(('groups', 'seed'), 'lat'), parts along dimension 0, may hold values from 9.9658966e-05 to 0.0099487305
Outputs:
- new_weight: bfloat16 [4, 16384, 2048], P(('groups', 'seed'), 'lat'), parts along dimension 0
- new_first: bfloat16 [4, 16384, 2048], P(('groups', 'seed'), 'lat'), parts along dimension 0
- new_second: bfloat16 [4, 16384, 2048], P(('groups', 'seed'), 'lat'), parts along dimension 0
There are 2 independent parts, one for each index of `groups`. A program takes and returns all parts, laid end to end along the dimension named above; each array names one. Nothing has to cross between parts.
All inputs are finite; a program needn't handle non-finite values. No bound on the sum of `keep_cols` on one device may be relied on, other than what follows from the above.
Results may differ from a plain program's by a relative error of at most 0.012.
The roundings to bfloat16 on the way count: a program that leaves them out, or rounds other values in their place, can miss the bound.
Values may be sent and summed in bfloat16 or wider, within the bound.
No kernel may reach another device: no remote copies, remote signals or barrier semaphores. Data moves between devices by JAX's collectives and lax.ppermute only.
A program may use at most 128 MiB of HBM per device.

v0:
```python
import jax
import jax.numpy as jnp
from jax import lax
from jax.sharding import PartitionSpec as P

sparsity = 0.2
beta_one = 0.9
beta_two = 0.95
corr_one = 1.0 - 0.9**10
corr_two = 1.0 - 0.95**10
adam_eps = 1e-08
rate_step = 0.001
decay_rate = 0.1


def local(
    activations,
    bag_rows,
    keep_cols,
    enc_weight,
    enc_bias,
    dec_weight,
    dec_bias,
    first_moment,
    second_moment,
):
    half_rows = lax.all_gather(activations, "lat", axis=1, tiled=True)
    gathered = lax.all_gather(half_rows, "seed", axis=0, tiled=True)
    row_order = bag_rows[0]
    sample = jnp.take(gathered, row_order, axis=0)
    weight_in = enc_weight[0]
    decoder = dec_weight[0]
    bias_dec = dec_bias[0]
    keep = keep_cols[0].astype(jnp.float32)
    centered = (sample.astype(jnp.float32) - bias_dec).astype(jnp.bfloat16)
    pre_t = lax.dot_general(
        weight_in, centered, (((1,), (1,)), ((), ())), preferred_element_type=jnp.float32
    )
    pre_t = pre_t + enc_bias[0][:, None]
    latent_t = jnp.maximum(pre_t, 0.0).astype(jnp.bfloat16)
    partial_sum = lax.dot_general(
        latent_t, decoder, (((0,), (0,)), ((), ())), preferred_element_type=jnp.float32
    )
    total = lax.psum(partial_sum, "lat")
    error = ((total + bias_dec - sample.astype(jnp.float32)) * keep).astype(jnp.bfloat16)
    back_t = lax.dot_general(
        decoder, error, (((1,), (1,)), ((), ())), preferred_element_type=jnp.float32
    )
    row_norm = jnp.sqrt(jnp.sum(jnp.square(decoder.astype(jnp.float32)), axis=1) + 1e-06)
    token_total = sample.shape[0]
    d_pre_t = (
        jnp.where(pre_t > 0, 2.0 * back_t + sparsity * row_norm[:, None], 0.0) / token_total
    ).astype(jnp.bfloat16)
    grad = jnp.dot(d_pre_t, centered, preferred_element_type=jnp.float32)
    moment_one = beta_one * first_moment[0].astype(jnp.float32) + (1.0 - beta_one) * grad
    moment_two = beta_two * second_moment[0].astype(jnp.float32) + (1.0 - beta_two) * grad * grad
    direction = moment_one / corr_one / (jnp.sqrt(moment_two / corr_two) + adam_eps)
    old = weight_in.astype(jnp.float32)
    updated = (old - rate_step * (direction + decay_rate * old)).astype(jnp.bfloat16)
    return (
        updated[None],
        moment_one.astype(jnp.bfloat16)[None],
        moment_two.astype(jnp.bfloat16)[None],
    )


def solution(mesh):
    return jax.shard_map(
        local,
        mesh=mesh,
        in_specs=(
            P(("groups", "seed"), "lat"),
            P(("groups", "seed"), None),
            P(("groups", "seed"), None),
            P(("groups", "seed"), "lat", None),
            P(("groups", "seed"), "lat"),
            P(("groups", "seed"), "lat", None),
            P(("groups", "seed"), None),
            P(("groups", "seed"), "lat", None),
            P(("groups", "seed"), "lat", None),
        ),
        out_specs=(
            P(("groups", "seed"), "lat", None),
            P(("groups", "seed"), "lat", None),
            P(("groups", "seed"), "lat", None),
        ),
        check_vma=False,
    )
```

profile of v0, /device:TPU:0, one launch (start us, length us, event | category | flops | bytes accessed | tf_op | source)
XLA Modules:
  0.0 222.0 jit_solution(16715430085450274316)
XLA Ops:
  7.2 0.0 copy-start
  7.2 0.0 copy-start.2
  7.2 0.0 all-gather.2.cloned.1.call-start
  7.2 35.4 %all_gather.6 = bf16[128,2048]{1,0:T(8,128)(2,1)} all-gather(bf16[128,256]{1,0:T(8,128)(2,1)} %param.9), channel_id=1, replica_groups=mesh['groups'=2,'lat'=8,'seed'=2] {'lat'}, dimensions={1}, use_global_device_ids=true | all-gather | bytes 589824 | tf_op jit(solution)/shard_map/all_gather | solution.py:27
  42.6 0.0 all-gather.2.cloned.1.call-update
  42.7 0.0 all-reduce.2.cloned.1.call-start
  42.7 0.7 compare_select_fusion
  43.4 0.7 compare_and_fusion
  44.1 8.8 %all-gather.2.cloned.1.call-done = bf16[256,2048]{1,0:T(8,128)(2,1)} async-done(((bf16[128,2048]{1,0:T(8,128)(2,1)}), bf16[256,2048]{1,0:T(8,128)(2,1)}) %all-gather.2.cloned.1.call-update) | async-done | bytes 1048592 | tf_op jit(solution)/shard_map/all_gather | solution.py:28
  52.9 3.7 %gather_fusion = bf16[256,2048]{1,0:T(8,128)(2,1)S(1)} fusion(bf16[256,2048]{1,0:T(8,128)(2,1)} %all-gather.2.cloned.1.call-done, s32[1024]{0:T(1024)S(1)} %pad_clamp_fusion), kind=kCustom, calls=%fused_computation | custom fusion | bytes 2098176 | tf_op jit(solution)/shard_map/jit(_take)/gather | solution.py:30
  56.6 0.0 copy-done
  56.6 0.0 copy-done.2
  56.7 5.8 %fusion.27 = f32[256,2048]{1,0:T(8,128)S(1)} fusion(bf16[1,2048,2048]{2,1,0:T(8,128)(2,1)} %param.12, f32[2048]{0:T(1024)S(1)} %bitcast.64, f32[2048]{0:T(1024)S(1)} %bitcast.59, bf16[256,2048]{1,0:T(8,128)(2,1)S(1)} %gather_fusion, pred[256]{0:T(512)(128)(4,1)S(1)} %compare_and_fusion), kind=kOutput, calls=%fused_computation.27 | convolution fusion | flops 2150105088 | bytes 11550976 | tf_op jit(solution)/shard_map/dot_general | solution.py:36
  62.4 0.0 copy-start.1
  62.5 7.0 %fusion.10 = f32[256,2048]{1,0:T(8,128)} fusion(bf16[1,2048,2048]{2,1,0:T(8,128)(2,1)} %param.14, f32[256,2048]{1,0:T(8,128)S(1)} %fusion.27), kind=kOutput, calls=%fused_computation.16 | convolution fusion | flops 2148532224 | bytes 12582912 | tf_op jit(solution)/shard_map/dot_general | solution.py:41
  69.5 0.0 all-reduce.2.cloned.1.call-update
  69.5 0.0 copy-done.1
  69.5 5.1 %multiply_reduce_fusion = f32[2048]{0:T(1024)S(1)} fusion(bf16[1,2048,2048]{2,1,0:T(8,128)(2,1)} %param.14), kind=kLoop, calls=%fused_computation.9 | loop fusion | flops 12580864 | bytes 8396800 | tf_op jit(solution)/shard_map/reduce_sum | solution.py:49
  74.6 98.0 %all-reduce.2.cloned.1.call-done = f32[256,2048]{1,0:T(8,128)} async-done(((f32[256,2048]{1,0:T(8,128)}), f32[256,2048]{1,0:T(8,128)}) %all-reduce.2.cloned.1.call-update) | async-done | bytes 2097168 | tf_op jit(solution)/shard_map/psum | solution.py:44
  172.7 14.7 %fusion.34 = f32[2048,2048]{1,0:T(8,128)} fusion(bf16[1,2048,2048]{2,1,0:T(8,128)(2,1)} %param.14, f32[256,2048]{1,0:T(8,128)S(1)} %fusion.27, f32[256,2048]{1,0:T(8,128)} %all-reduce.2.cloned.1.call-done, f32[2048]{0:T(1024)S(1)} %sqrt_multiply_fusion, f32[2048]{0:T(1024)S(1)} %bitcast.61, f32[2048]{0:T(1024)S(1)} %bitcast.60, ...), kind=kOutput, calls=%fused_computation.29 | convolution fusion | flops 4303355904 | bytes 30433536 | tf_op jit(solution)/shard_map/dot_general | solution.py:54
  187.3 27.9 %fusion.6 = (bf16[1,2048,2048]{2,1,0:T(8,128)(2,1)}, bf16[1,2048,2048]{2,1,0:T(8,128)(2,1)}, bf16[1,2048,2048]{2,1,0:T(8,128)(2,1)}) fusion(f32[2048,2048]{1,0:T(8,128)} %fusion.34, bf16[1,2048,2048]{2,1,0:T(8,128)(2,1)} %param.17, bf16[1,2048,2048]{2,1,0:T(8,128)(2,1)} %param.16, bf16[1,2048,2048]{2,1,0:T(8,128)(2,1)} %param.12), kind=kLoop, calls=%fused_computation.12 | loop fusion | flops 88080384 | bytes 67108864 | tf_op jit(solution)/shard_map/broadcast_in_dim | solution.py:63
  (3 shorter events, 0.0 us)
Async XLA Ops:
  7.2 49.5 %copy-start = (f32[1,2048]{1,0:T(1,128)S(1)}, f32[1,2048]{1,0:T(1,128)}, u32[]{:S(2)}) copy-start(f32[1,2048]{1,0:T(1,128)} %param.15) | copy-start | bytes 24580
  7.2 49.5 %copy-start.2 = (f32[1,2048]{1,0:T(1,128)S(1)}, f32[1,2048]{1,0:T(1,128)}, u32[]{:S(2)}) copy-start(f32[1,2048]{1,0:T(1,128)} %param.13) | copy-start | bytes 24580
  7.2 45.7 %all-gather.2.cloned.1.call-start = ((), (), s32[]{:S(2)}) async-start(), calls=%async_computation | async-start | bytes 1572864 | tf_op jit(solution)/shard_map/all_gather | solution.py:28
  42.7 130.0 %all-reduce.2.cloned.1.call-start = ((), (), s32[]{:S(2)}) async-start(), calls=%async_computation.1 | async-start | bytes 4194304 | tf_op jit(solution)/shard_map/psum | solution.py:44
  62.4 7.1 %copy-start.1 = (s32[1,2048]{1,0:T(1,128)S(1)}, s32[1,2048]{1,0:T(1,128)}, u32[]{:S(2)}) copy-start(s32[1,2048]{1,0:T(1,128)} %param.11) | copy-start | bytes 24580
Sparse Core Ops, SparseCore 0:
  42.8 10.0 all-gather.1
  69.6 103.0 all-reduce.1
where the time goes:
time: 222 us
  waiting for transfers between devices  107 us (48%)
  blocking collectives  35.4 us (16%)
  other arithmetic  34.3 us (15%)
  matrix products  27.5 us (12%)
  between operations  14.1 us (6%)
  local copies, waits for them, and re-layouts  3.74 us (2%)
    psum x1, waiting for transfers between devices, local(): total = lax.psum(partial_sum, 'lat')  98 us
    all_gather x1, blocking collectives, local(): half_rows = lax.all_gather(activations, 'lat', axis=1, tiled=True)  35.4 us
    broadcast_in_dim x1, other arithmetic, local(): moment_two.astype(jnp.bfloat16)[None]  27.9 us
    dot_general x1, matrix products, local(): grad = jnp.dot(d_pre_t, centered, preferred_element_type=jnp.float32)  14.7 us
    all_gather x1, waiting for transfers between devices, local(): gathered = lax.all_gather(half_rows, 'seed', axis=0, tiled=True)  8.8 us
    dot_general x1, matrix products, local(): lax.dot_general(latent_t, decoder, (((0,), (0,)), ((), ())), preferred_el...  7.04 us
    dot_general x1, matrix products, local(): lax.dot_general(weight_in, centered, (((1,), (1,)), ((), ())), preferred_...  5.77 us
    reduce_sum x1, other arithmetic, local(): jnp.sum(jnp.square(decoder.astype(jnp.float32)), axis=1) + 1e-06  5.08 us
  transfers between devices with their start and end apart: 2, of which 2 were waited for; matrix products, arithmetic and copies ran while one was open for 3% of the time, Pallas kernels for 0%

commit v1 on v0

--- a/solution.py
+++ b/solution.py
@@ -2,6 +2,7 @@
 import jax.numpy as jnp
 from jax import lax
 from jax.sharding import PartitionSpec as P
+from jax.lax import axis_index, axis_size, ppermute
 
 sparsity = 0.2
 beta_one = 0.9
@@ -24,7 +25,17 @@
     first_moment,
     second_moment,
 ):
-    half_rows = lax.all_gather(activations, "lat", axis=1, tiled=True)
+    shares = axis_size("lat")
+    last = sorted(((src_i, (src_i + 1) % shares) for src_i in range(shares)))
+    kept_arr = activations
+    rows = [kept_arr]
+    for s in range(1, shares):
+        kept_arr = ppermute(kept_arr, "lat", last)
+        rows.insert(0, kept_arr)
+    y1 = jnp.concatenate(rows, axis=1)
+    view_out = axis_index("lat")
+    part_next = view_out + 1
+    half_rows = jnp.roll(y1, part_next * activations.shape[1], 1)
     gathered = lax.all_gather(half_rows, "seed", axis=0, tiled=True)
     row_order = bag_rows[0]
     sample = jnp.take(gathered, row_order, axis=0)

time: 222 us -> 237 us (1.068)
  waiting for transfers between devices: 107 us -> 151 us
  blocking collectives: 35.4 us -> 0 us
  starting transfers between devices: 0.08 us -> 3.09 us
  local copies, waits for them, and re-layouts: 3.74 us -> 6.36 us
    ppermute x0 -> x7, waiting for transfers between devices: none -> 47.7 us  [local(): kept_arr = ppermute(kept_arr, 'lat', last)]
    all_gather x1 -> x0, blocking collectives: 35.4 us -> none  [local(): half_rows = lax.all_gather(activations, 'lat', axis=1, tiled=True)]
    all_gather x1, waiting for transfers between devices: 8.8 us -> 5.33 us  [local(): gathered = lax.all_gather(half_rows, 'seed', axis=0, tiled=True)]
    ppermute x0 -> x7, starting transfers between devices: none -> 3.01 us  [local(): kept_arr = ppermute(kept_arr, 'lat', last)]
  transfers between devices with their start and end apart: 2 -> 9, of which waited for: 2 -> 9; matrix products, arithmetic and copies ran while one was open for 3% -> 3% of each run, Pallas kernels for 0% -> 0%
where the time goes in v1:
time: 237 us
  waiting for transfers between devices  151 us (64%)
  other arithmetic  34.3 us (14%)
  matrix products  27.5 us (12%)
  between operations  14.2 us (6%)
  local copies, waits for them, and re-layouts  6.36 us (3%)
  starting transfers between devices  3.09 us (1%)
    psum x1, waiting for transfers between devices, local(): total = lax.psum(partial_sum, 'lat')  98 us
    ppermute x7, waiting for transfers between devices, local(): kept_arr = ppermute(kept_arr, 'lat', last)  47.7 us
    broadcast_in_dim x1, other arithmetic, local(): moment_two.astype(jnp.bfloat16)[None]  27.9 us
    dot_general x1, matrix products, local(): grad = jnp.dot(d_pre_t, centered, preferred_element_type=jnp.float32)  14.7 us
    dot_general x1, matrix products, local(): lax.dot_general(latent_t, decoder, (((0,), (0,)), ((), ())), preferred_el...  7.04 us
    dot_general x1, matrix products, local(): lax.dot_general(weight_in, centered, (((1,), (1,)), ((), ())), preferred_...  5.77 us
    all_gather x1, waiting for transfers between devices, local(): gathered = lax.all_gather(half_rows, 'seed', axis=0, tiled=True)  5.33 us
    reduce_sum x1, other arithmetic, local(): jnp.sum(jnp.square(decoder.astype(jnp.float32)), axis=1) + 1e-06  5.08 us
  transfers between devices with their start and end apart: 9, of which 9 were waited for; matrix products, arithmetic and copies ran while one was open for 3% of the time, Pallas kernels for 0%

profile of v1, /device:TPU:0, one launch (start us, length us, event | category | flops | bytes accessed | tf_op | source)
XLA Modules:
  0.0 236.6 jit_solution(8966899415361152966)
XLA Ops:
  7.2 0.0 all-gather.2.cloned.1.call-start
  7.2 3.0 %collective-permute-start = (bf16[128,256]{1,0:T(8,128)(2,1)}, bf16[128,256]{1,0:T(8,128)(2,1)S(1)}, u32[]{:S(2)}, u32[]{:S(2)}) collective-permute-start(bf16[128,256]{1,0:T(8,128)(2,1)} %param.9), channel_id=1, source_target_pairs={{0,2},{2,4},{4,6},{6,8},{8,10},{10,12},{12,14},{14,0},{1,3},{3,5},... | collective-permute-start | bytes 196616 | tf_op jit(solution)/shard_map/ppermute | solution.py:33
  10.2 5.5 %collective-permute-done = bf16[128,256]{1,0:T(8,128)(2,1)S(1)} collective-permute-done((bf16[128,256]{1,0:T(8,128)(2,1)}, bf16[128,256]{1,0:T(8,128)(2,1)S(1)}, u32[]{:S(2)}, u32[]{:S(2)}) %collective-permute-start) | collective-permute-done | bytes 65568 | tf_op jit(solution)/shard_map/ppermute | solution.py:33
  15.7 0.0 collective-permute-start.1
  15.7 7.0 %collective-permute-done.1 = bf16[128,256]{1,0:T(8,128)(2,1)S(1)} collective-permute-done((bf16[128,256]{1,0:T(8,128)(2,1)S(1)}, bf16[128,256]{1,0:T(8,128)(2,1)S(1)}, u32[]{:S(2)}, u32[]{:S(2)}) %collective-permute-start.1) | collective-permute-done | bytes 65568 | tf_op jit(solution)/shard_map/ppermute | solution.py:33
  22.7 0.0 collective-permute-start.2
  22.7 7.0 %collective-permute-done.2 = bf16[128,256]{1,0:T(8,128)(2,1)S(1)} collective-permute-done((bf16[128,256]{1,0:T(8,128)(2,1)S(1)}, bf16[128,256]{1,0:T(8,128)(2,1)S(1)}, u32[]{:S(2)}, u32[]{:S(2)}) %collective-permute-start.2) | collective-permute-done | bytes 65568 | tf_op jit(solution)/shard_map/ppermute | solution.py:33
  29.6 0.0 collective-permute-start.3
  29.6 7.0 %collective-permute-done.3 = bf16[128,256]{1,0:T(8,128)(2,1)S(1)} collective-permute-done((bf16[128,256]{1,0:T(8,128)(2,1)S(1)}, bf16[128,256]{1,0:T(8,128)(2,1)S(1)}, u32[]{:S(2)}, u32[]{:S(2)}) %collective-permute-start.3) | collective-permute-done | bytes 65568 | tf_op jit(solution)/shard_map/ppermute | solution.py:33
  36.6 0.0 collective-permute-start.4
  36.6 7.4 %collective-permute-done.4 = bf16[128,256]{1,0:T(8,128)(2,1)S(1)} collective-permute-done((bf16[128,256]{1,0:T(8,128)(2,1)S(1)}, bf16[128,256]{1,0:T(8,128)(2,1)S(1)}, u32[]{:S(2)}, u32[]{:S(2)}) %collective-permute-start.4) | collective-permute-done | bytes 65568 | tf_op jit(solution)/shard_map/ppermute | solution.py:33
  44.0 0.0 collective-permute-start.5
  44.0 7.0 %collective-permute-done.5 = bf16[128,256]{1,0:T(8,128)(2,1)S(1)} collective-permute-done((bf16[128,256]{1,0:T(8,128)(2,1)S(1)}, bf16[128,256]{1,0:T(8,128)(2,1)S(1)}, u32[]{:S(2)}, u32[]{:S(2)}) %collective-permute-start.5) | collective-permute-done | bytes 65568 | tf_op jit(solution)/shard_map/ppermute | solution.py:33
  51.0 0.0 collective-permute-start.6
  51.0 7.0 %collective-permute-done.6 = bf16[128,256]{1,0:T(8,128)(2,1)S(1)} collective-permute-done((bf16[128,256]{1,0:T(8,128)(2,1)S(1)}, bf16[128,256]{1,0:T(8,128)(2,1)S(1)}, u32[]{:S(2)}, u32[]{:S(2)}) %collective-permute-start.6) | collective-permute-done | bytes 65568 | tf_op jit(solution)/shard_map/ppermute | solution.py:33
  58.0 0.8 constant_dynamic-update-slice_fusion.8
  59.0 0.8 constant_dynamic-update-slice_fusion
  59.8 0.8 constant_dynamic-slice_fusion
  60.6 0.0 all-gather.2.cloned.1.call-update
  60.7 0.0 all-reduce.2.cloned.1.call-start
  60.7 0.7 compare_select_fusion
  61.4 0.7 compare_and_fusion
  62.1 5.3 %all-gather.2.cloned.1.call-done = bf16[256,2048]{1,0:T(8,128)(2,1)} async-done(((bf16[128,2048]{1,0:T(8,128)(2,1)}), bf16[256,2048]{1,0:T(8,128)(2,1)}) %all-gather.2.cloned.1.call-update) | async-done | bytes 1048592 | tf_op jit(solution)/shard_map/all_gather | solution.py:39
  67.4 3.7 %gather_fusion = bf16[256,2048]{1,0:T(8,128)(2,1)S(1)} fusion(bf16[256,2048]{1,0:T(8,128)(2,1)} %all-gather.2.cloned.1.call-done, s32[1024]{0:T(1024)S(1)} %pad_clamp_fusion), kind=kCustom, calls=%fused_computation | custom fusion | bytes 2098176 | tf_op jit(solution)/shard_map/jit(_take)/gather | solution.py:41
  71.2 5.8 %fusion.27 = f32[256,2048]{1,0:T(8,128)S(1)} fusion(bf16[1,2048,2048]{2,1,0:T(8,128)(2,1)} %param.12, f32[2048]{0:T(1024)S(1)} %bitcast.64, f32[2048]{0:T(1024)S(1)} %bitcast.59, bf16[256,2048]{1,0:T(8,128)(2,1)S(1)} %gather_fusion, pred[256]{0:T(512)(128)(4,1)S(1)} %compare_and_fusion), kind=kOutput, calls=%fused_computation.27 | convolution fusion | flops 2150105088 | bytes 11550976 | tf_op jit(solution)/shard_map/dot_general | solution.py:47
  77.0 0.0 copy-start.1
  77.0 7.0 %fusion.10 = f32[256,2048]{1,0:T(8,128)} fusion(bf16[1,2048,2048]{2,1,0:T(8,128)(2,1)} %param.14, f32[256,2048]{1,0:T(8,128)S(1)} %fusion.27), kind=kOutput, calls=%fused_computation.16 | convolution fusion | flops 2148532224 | bytes 12582912 | tf_op jit(solution)/shard_map/dot_general | solution.py:52
  84.0 0.0 all-reduce.2.cloned.1.call-update
  84.1 5.1 %multiply_reduce_fusion = f32[2048]{0:T(1024)S(1)} fusion(bf16[1,2048,2048]{2,1,0:T(8,128)(2,1)} %param.14), kind=kLoop, calls=%fused_computation.9 | loop fusion | flops 12580864 | bytes 8396800 | tf_op jit(solution)/shard_map/reduce_sum | solution.py:60
  89.2 98.0 %all-reduce.2.cloned.1.call-done = f32[256,2048]{1,0:T(8,128)} async-done(((f32[256,2048]{1,0:T(8,128)}), f32[256,2048]{1,0:T(8,128)}) %all-reduce.2.cloned.1.call-update) | async-done | bytes 2097168 | tf_op jit(solution)/shard_map/psum | solution.py:55
  187.2 14.7 %fusion.34 = f32[2048,2048]{1,0:T(8,128)} fusion(bf16[1,2048,2048]{2,1,0:T(8,128)(2,1)} %param.14, f32[256,2048]{1,0:T(8,128)S(1)} %fusion.27, f32[256,2048]{1,0:T(8,128)} %all-reduce.2.cloned.1.call-done, f32[2048]{0:T(1024)S(1)} %sqrt_multiply_fusion, f32[2048]{0:T(1024)S(1)} %bitcast.61, f32[2048]{0:T(1024)S(1)} %bitcast.60, ...), kind=kOutput, calls=%fused_computation.29 | convolution fusion | flops 4303355904 | bytes 30433536 | tf_op jit(solution)/shard_map/dot_general | solution.py:65
  201.9 27.9 %fusion.6 = (bf16[1,2048,2048]{2,1,0:T(8,128)(2,1)}, bf16[1,2048,2048]{2,1,0:T(8,128)(2,1)}, bf16[1,2048,2048]{2,1,0:T(8,128)(2,1)}) fusion(f32[2048,2048]{1,0:T(8,128)} %fusion.34, bf16[1,2048,2048]{2,1,0:T(8,128)(2,1)} %param.17, bf16[1,2048,2048]{2,1,0:T(8,128)(2,1)} %param.16, bf16[1,2048,2048]{2,1,0:T(8,128)(2,1)} %param.12), kind=kLoop, calls=%fused_computation.12 | loop fusion | flops 88080384 | bytes 67108864 | tf_op jit(solution)/shard_map/broadcast_in_dim | solution.py:74
  (22 shorter events, 0.1 us)
Async XLA Ops:
  7.2 64.0 %copy-start = (f32[1,2048]{1,0:T(1,128)S(1)}, f32[1,2048]{1,0:T(1,128)}, u32[]{:S(2)}) copy-start(f32[1,2048]{1,0:T(1,128)} %param.15) | copy-start | bytes 24580
  7.2 64.0 %copy-start.2 = (f32[1,2048]{1,0:T(1,128)S(1)}, f32[1,2048]{1,0:T(1,128)}, u32[]{:S(2)}) copy-start(f32[1,2048]{1,0:T(1,128)} %param.13) | copy-start | bytes 24580
  7.2 60.2 %all-gather.2.cloned.1.call-start = ((), (), s32[]{:S(2)}) async-start(), calls=%async_computation | async-start | bytes 1572864 | tf_op jit(solution)/shard_map/all_gather | solution.py:39
  7.2 8.5 %collective-permute-start = (bf16[128,256]{1,0:T(8,128)(2,1)}, bf16[128,256]{1,0:T(8,128)(2,1)S(1)}, u32[]{:S(2)}, u32[]{:S(2)}) collective-permute-start(bf16[128,256]{1,0:T(8,128)(2,1)} %param.9), channel_id=1, source_target_pairs={{0,2},{2,4},{4,6},{6,8},{8,10},{10,12},{12,14},{14,0},{1,3},{3,5},... | collective-permute-start | bytes 196616 | tf_op jit(solution)/shard_map/ppermute | solution.py:33
  15.7 7.0 %collective-permute-start.1 = (bf16[128,256]{1,0:T(8,128)(2,1)S(1)}, bf16[128,256]{1,0:T(8,128)(2,1)S(1)}, u32[]{:S(2)}, u32[]{:S(2)}) collective-permute-start(bf16[128,256]{1,0:T(8,128)(2,1)S(1)} %collective-permute-done), channel_id=1, source_target_pairs={{0,2},{2,4},{4,6},{6,8},{8,10},{10,12},{12,14},{14,0},{1,3},{3,5},... | collective-permute-start | bytes 196616 | tf_op jit(solution)/shard_map/ppermute | solution.py:33
  22.7 7.0 %collective-permute-start.2 = (bf16[128,256]{1,0:T(8,128)(2,1)S(1)}, bf16[128,256]{1,0:T(8,128)(2,1)S(1)}, u32[]{:S(2)}, u32[]{:S(2)}) collective-permute-start(bf16[128,256]{1,0:T(8,128)(2,1)S(1)} %collective-permute-done.1), channel_id=1, source_target_pairs={{0,2},{2,4},{4,6},{6,8},{8,10},{10,12},{12,14},{14,0},{1,3},{3,5},... | collective-permute-start | bytes 196616 | tf_op jit(solution)/shard_map/ppermute | solution.py:33
  29.6 7.0 %collective-permute-start.3 = (bf16[128,256]{1,0:T(8,128)(2,1)S(1)}, bf16[128,256]{1,0:T(8,128)(2,1)S(1)}, u32[]{:S(2)}, u32[]{:S(2)}) collective-permute-start(bf16[128,256]{1,0:T(8,128)(2,1)S(1)} %collective-permute-done.2), channel_id=1, source_target_pairs={{0,2},{2,4},{4,6},{6,8},{8,10},{10,12},{12,14},{14,0},{1,3},{3,5},... | collective-permute-start | bytes 196616 | tf_op jit(solution)/shard_map/ppermute | solution.py:33
  36.6 7.4 %collective-permute-start.4 = (bf16[128,256]{1,0:T(8,128)(2,1)S(1)}, bf16[128,256]{1,0:T(8,128)(2,1)S(1)}, u32[]{:S(2)}, u32[]{:S(2)}) collective-permute-start(bf16[128,256]{1,0:T(8,128)(2,1)S(1)} %collective-permute-done.3), channel_id=1, source_target_pairs={{0,2},{2,4},{4,6},{6,8},{8,10},{10,12},{12,14},{14,0},{1,3},{3,5},... | collective-permute-start | bytes 196616 | tf_op jit(solution)/shard_map/ppermute | solution.py:33
  44.0 7.0 %collective-permute-start.5 = (bf16[128,256]{1,0:T(8,128)(2,1)S(1)}, bf16[128,256]{1,0:T(8,128)(2,1)S(1)}, u32[]{:S(2)}, u32[]{:S(2)}) collective-permute-start(bf16[128,256]{1,0:T(8,128)(2,1)S(1)} %collective-permute-done.4), channel_id=1, source_target_pairs={{0,2},{2,4},{4,6},{6,8},{8,10},{10,12},{12,14},{14,0},{1,3},{3,5},... | collective-permute-start | bytes 196616 | tf_op jit(solution)/shard_map/ppermute | solution.py:33
  51.0 7.0 %collective-permute-start.6 = (bf16[128,256]{1,0:T(8,128)(2,1)S(1)}, bf16[128,256]{1,0:T(8,128)(2,1)S(1)}, u32[]{:S(2)}, u32[]{:S(2)}) collective-permute-start(bf16[128,256]{1,0:T(8,128)(2,1)S(1)} %collective-permute-done.5), channel_id=1, source_target_pairs={{0,2},{2,4},{4,6},{6,8},{8,10},{10,12},{12,14},{14,0},{1,3},{3,5},... | collective-permute-start | bytes 196616 | tf_op jit(solution)/shard_map/ppermute | solution.py:33
  60.7 126.5 %all-reduce.2.cloned.1.call-start = ((), (), s32[]{:S(2)}) async-start(), calls=%async_computation.1 | async-start | bytes 4194304 | tf_op jit(solution)/shard_map/psum | solution.py:55
  77.0 7.1 %copy-start.1 = (s32[1,2048]{1,0:T(1,128)S(1)}, s32[1,2048]{1,0:T(1,128)}, u32[]{:S(2)}) copy-start(s32[1,2048]{1,0:T(1,128)} %param.11) | copy-start | bytes 24580
Sparse Core Ops, SparseCore 0:
  60.8 6.5 all-gather.1
  84.2 103.0 all-reduce.1
